TPU v7x, 256 devices: a whole 4x4x8 slice. The times are simulated.
256 devices in a mesh: dp: 16 (over z_lo, x), block: 16 (over z_hi, y, core).
Axes of the slice: x: 4, y: 4, z: 8 (z_hi: 2, z_lo: 4; z = z_hi * 4 + z_lo), core: 2. Of those that a mesh axis runs over, the one named last changes fastest.
Arguments:
- inputs: bfloat16 [6144, 8192], P('dp', 'block'), may hold values from -6 to 6
- weight_in: bfloat16 [512, 5, 16384], P('dp', None, 'block'), may hold values from -0.125 to 0.125
- weight_out: bfloat16 [1024, 5, 8192], P('dp', None, 'block'), may hold values from -0.078125 to 0.078125
- cotangent: bfloat16 [6144, 8192], P('dp', 'block'), may hold values from -6 to 6
Outputs:
- outputs: bfloat16 [6144, 8192], P('dp', 'block')
- input_grad: bfloat16 [6144, 8192], P('dp', 'block')
- grad_in: float32 [512, 5, 16384], P('dp', None, 'block')
- grad_out: float32 [1024, 5, 8192], P('dp', None, 'block')
All inputs are finite; a program needn't handle non-finite values.
Results may differ from a plain program's by a relative error of at most 0.017.
Values may be sent and summed in bfloat16 or wider, within the bound.
No kernel may reach another device: no remote copies, remote signals or barrier semaphores. Data moves between devices by JAX's collectives and lax.ppermute only.
A program may use at most 128 MiB of HBM per device.

v0:
```python
import jax
import jax.numpy as jnp
from jax import lax
from jax.sharding import PartitionSpec as P


def swapped(value, axis, distance):
    mask = 2**distance
    pairs = [(source, source ^ mask) for source in range(lax.axis_size(axis))]
    return lax.ppermute(value, axis, pairs)


def gelu_tanh(value):
    return jax.nn.gelu(value, approximate=True)


def rounded(value):
    return lax.optimization_barrier(value.astype(jnp.bfloat16)).astype(jnp.float32)


def reduce_in(in_stack, pre_grad, shard_rows):

    def term(start, count):
        return jnp.einsum("tkc,th->ckh", in_stack, pre_grad, preferred_element_type=jnp.float32)

    return lax.psum_scatter(
        term(jnp.int32(0), lax.axis_size("dp") * shard_rows).astype(jnp.bfloat16),
        "dp",
        scatter_dimension=0,
        tiled=True,
    ).astype(jnp.float32)


def reduce_out(hid_stack, cotangent, shard_rows):

    def term(start, count):
        return jnp.einsum("tkh,tc->hkc", hid_stack, cotangent, preferred_element_type=jnp.float32)

    return lax.psum_scatter(
        term(jnp.int32(0), lax.axis_size("dp") * shard_rows).astype(jnp.bfloat16),
        "dp",
        scatter_dimension=0,
        tiled=True,
    ).astype(jnp.float32)


def body(inputs, weight_in, weight_out, cotangent):
    levels = lax.axis_size("block").bit_length() - 1
    weight_in_all, weight_out_all = (
        lax.all_gather(weight_in, "dp", axis=0, tiled=True),
        lax.all_gather(weight_out, "dp", axis=0, tiled=True),
    )
    pieces = [inputs]
    for level_bit in range(levels):
        pieces.append(swapped(inputs, "block", level_bit))
    in_stack = jnp.stack(pieces, axis=1)
    pre_act = jnp.einsum("tkc,ckh->th", in_stack, weight_in_all, preferred_element_type=jnp.float32)
    hidden = gelu_tanh(pre_act).astype(jnp.bfloat16)
    hid_pieces = [hidden]
    for level_bit in range(levels):
        hid_pieces.append(swapped(hidden, "block", level_bit))
    hid_stack = jnp.stack(hid_pieces, axis=1)
    outputs = jnp.einsum(
        "tkh,hkc->tc", hid_stack, weight_out_all, preferred_element_type=jnp.float32
    ).astype(jnp.bfloat16)
    back_terms = jnp.einsum(
        "tc,hkc->tkh", cotangent, weight_out_all, preferred_element_type=jnp.float32
    )
    back_round = back_terms.astype(jnp.bfloat16)
    hid_grad = rounded(back_terms[:, 0, :])
    for level_bit in range(levels):
        arrived = swapped(back_round[:, level_bit + 1, :], "block", level_bit)
        hid_grad = hid_grad + arrived.astype(jnp.float32)
    slope = jax.vjp(gelu_tanh, pre_act)[1](hid_grad)[0]
    pre_grad = slope.astype(jnp.bfloat16)
    in_terms = jnp.einsum(
        "th,ckh->tkc", pre_grad, weight_in_all, preferred_element_type=jnp.float32
    )
    in_round = in_terms.astype(jnp.bfloat16)
    in_total = rounded(in_terms[:, 0, :])
    for level_bit in range(levels):
        arrived = swapped(in_round[:, level_bit + 1, :], "block", level_bit)
        in_total = in_total + arrived.astype(jnp.float32)
    input_grad = in_total.astype(jnp.bfloat16)
    grad_in = reduce_in(in_stack, pre_grad, weight_in.shape[0])
    grad_out = reduce_out(hid_stack, cotangent, weight_out.shape[0])
    return (outputs, input_grad, grad_in, grad_out)


def solution(mesh):
    placed = (P("dp", "block"), P("dp", None, "block"), P("dp", None, "block"), P("dp", "block"))
    return jax.shard_map(
        body,
        mesh=mesh,
        in_specs=placed,
        out_specs=(
            P("dp", "block"),
            P("dp", "block"),
            P("dp", None, "block"),
            P("dp", None, "block"),
        ),
        check_vma=False,
    )
```

profile of v0, /device:TPU:8, one launch (start us, length us, event | category | flops | bytes accessed | tf_op | source)
XLA Modules:
  0.0 489.9 jit_solution(4013147169355985098)
XLA Ops:
  8.8 2.2 collective-permute-start.1
  11.9 7.2 %collective-permute-start.3 = (bf16[384,512]{1,0:T(8,128)(2,1)}, bf16[384,512]{1,0:T(8,128)(2,1)}, u32[]{:S(2)}, u32[]{:S(2)}) collective-permute-start(bf16[384,512]{1,0:T(8,128)(2,1)} %param.4), channel_id=1, source_target_pairs={{0,8},{1,9},{2,10},{3,11},{4,12},{5,13},{6,14},{7,15},{8,0},{9,1},... | collective-permute-start | bytes 1179656 | tf_op jit(solution)/shard_map/ppermute | solution.py:10
  19.1 1.8 bitcast_dynamic-update-slice_fusion.9
  22.5 7.5 %collective-permute-done.2 = bf16[384,512]{1,0:T(8,128)(2,1)S(1)} collective-permute-done((bf16[384,512]{1,0:T(8,128)(2,1)}, bf16[384,512]{1,0:T(8,128)(2,1)S(1)}, u32[]{:S(2)}, u32[]{:S(2)}) %collective-permute-start.2) | collective-permute-done | bytes 393248 | tf_op jit(solution)/shard_map/ppermute | solution.py:10
  30.8 80.7 %all-gather.5.cloned.1.call-done = bf16[1024,5,512]{2,0,1:T(8,128)(2,1)} async-done(((bf16[64,5,512]{2,0,1:T(8,128)(2,1)}), bf16[1024,5,512]{2,0,1:T(8,128)(2,1)}) %all-gather.5.cloned.1.call-update) | async-done | bytes 5242896 | tf_op jit(solution)/shard_map/all_gather | solution.py:51
  111.4 4.7 convert_bitcast_fusion.2
  116.2 1.8 slice_bitcast_fusion.4
  117.9 3.5 collective-permute-start.11
  121.4 2.3 collective-permute-start.10
  123.7 2.5 collective-permute-start.9
  126.2 1.8 bitcast_dynamic-update-slice_fusion.5
  128.0 83.3 %all-gather.3.cloned.1.call-done = bf16[512,5,1024]{2,0,1:T(8,128)(2,1)} async-done(((bf16[32,5,1024]{2,0,1:T(8,128)(2,1)}), bf16[512,5,1024]{2,0,1:T(8,128)(2,1)}) %all-gather.3.cloned.1.call-update) | async-done | bytes 5242896 | tf_op jit(solution)/shard_map/all_gather | solution.py:50
  211.3 6.8 %bitcast_dynamic-update-slice_fusion.4 = (bf16[384,5,1024]{2,0,1:T(8,128)(2,1)}, bf16[384,1024]{1,0:T(8,128)(2,1)}, f32[384,1024,1]{1,0,2:T(8,128)S(1)}) fusion(bf16[384,5,512]{2,0,1:T(8,128)(2,1)} %bitcast_dynamic-update-slice_fusion.5, bf16[512,5,1024]{2,0,1:T(8,128)(2,1)} %all-gather.3.cloned.1.call-done), kind=kOutput, calls=%fused_computation.31 | convolution fusion | flops 2016804864 | bytes 10354688 | tf_op jit(solution)/shard_map/tkc,ckh->th/dot_general | solution.py:57
  219.0 2.9 fusion.6
  221.9 6.2 %convert_bitcast_fusion.1 = bf16[512,5,1024]{0,2,1:T(8,128)(2,1)} fusion(bf16[384,5,512]{2,0,1:T(8,128)(2,1)} %bitcast_dynamic-update-slice_fusion.5, bf16[384,1024]{1,0:T(8,128)(2,1)S(1)} %fusion.6), kind=kOutput, calls=%fused_computation.1 | convolution fusion | flops 2015887360 | bytes 7995392 | tf_op jit(solution)/shard_map/tkc,th->ckh/dot_general | solution.py:24
  228.1 11.9 %copy.14 = bf16[512,5,1024]{2,1,0:T(8,128)(2,1)} copy(bf16[512,5,1024]{0,2,1:T(8,128)(2,1)} %convert_bitcast_fusion.1) | data formatting | bytes 10485760 | tf_op jit(solution)/shard_map/convert_element_type | solution.py:27
  240.1 1.1 copy-done.3
  241.2 1.1 collective-permute-start.5
  243.0 3.8 collective-permute-start.7
  247.8 13.8 %collective-permute-done.5 = bf16[384,1024]{1,0:T(8,128)(2,1)S(1)} collective-permute-done((bf16[384,1024]{1,0:T(8,128)(2,1)S(1)}, bf16[384,1024]{1,0:T(8,128)(2,1)S(1)}, u32[]{:S(2)}, u32[]{:S(2)}) %collective-permute-start.5) | collective-permute-done | bytes 786464 | tf_op jit(solution)/shard_map/ppermute | solution.py:10
  262.5 15.2 %collective-permute-done.6 = bf16[384,1024]{1,0:T(8,128)(2,1)S(1)} collective-permute-done((bf16[384,1024]{1,0:T(8,128)(2,1)S(1)}, bf16[384,1024]{1,0:T(8,128)(2,1)S(1)}, u32[]{:S(2)}, u32[]{:S(2)}) %collective-permute-start.6) | collective-permute-done | bytes 786464 | tf_op jit(solution)/shard_map/ppermute | solution.py:10
  278.7 16.0 %collective-permute-done.7 = bf16[384,1024]{1,0:T(8,128)(2,1)S(1)} collective-permute-done((bf16[384,1024]{1,0:T(8,128)(2,1)S(1)}, bf16[384,1024]{1,0:T(8,128)(2,1)S(1)}, u32[]{:S(2)}, u32[]{:S(2)}) %collective-permute-start.7) | collective-permute-done | bytes 786464 | tf_op jit(solution)/shard_map/ppermute | solution.py:10
  295.7 6.8 %convert_bitcast_fusion = bf16[1024,5,512]{2,0,1:T(8,128)(2,1)} fusion(bf16[384,5,1024]{2,0,1:T(8,128)(2,1)} %bitcast_dynamic-update-slice_fusion, bf16[384,512]{1,0:T(8,128)(2,1)S(1)} %copy-done), kind=kOutput, calls=%fused_computation | convolution fusion | flops 2015887360 | bytes 9568256 | tf_op jit(solution)/shard_map/tkh,tc->hkc/dot_general | solution.py:37
  302.5 4.8 convert_bitcast_fusion.3
  307.5 4.8 collective-permute-start.15
  312.3 2.5 collective-permute-start.14
  315.1 5.5 %fusion.10 = bf16[384,512]{1,0:T(8,128)(2,1)} fusion(bf16[384,5,1024]{2,0,1:T(8,128)(2,1)S(1)} %copy-done.2, bf16[1024,5,512]{2,0,1:T(8,128)(2,1)} %all-gather.5.cloned.1.call-done), kind=kOutput, calls=%fused_computation.19 | convolution fusion | flops 2013462528 | bytes 9568256 | tf_op jit(solution)/shard_map/tkh,hkc->tc/dot_general | solution.py:63
  320.6 15.9 %collective-permute-done.15 = bf16[384,512]{1,0:T(8,128)(2,1)S(1)} collective-permute-done((bf16[384,512]{1,0:T(8,128)(2,1)S(1)}, bf16[384,512]{1,0:T(8,128)(2,1)S(1)}, u32[]{:S(2)}, u32[]{:S(2)}) %collective-permute-start.15) | collective-permute-done | bytes 393248 | tf_op jit(solution)/shard_map/ppermute | solution.py:10
  337.5 47.4 %reduce-scatter.3.cloned.1.call-done = bf16[32,5,1024]{2,1,0:T(8,128)(2,1)} async-done(((bf16[512,5,1024]{2,1,0:T(8,128)(2,1)}), bf16[32,5,1024]{2,1,0:T(8,128)(2,1)}) %reduce-scatter.3.cloned.1.call-update) | async-done | bytes 327696 | tf_op jit(solution)/shard_map/reduce_scatter | solution.py:26
  385.0 2.1 copy.16
  387.1 94.4 %reduce-scatter.5.cloned.1.call-done = bf16[64,5,512]{2,0,1:T(8,128)(2,1)} async-done(((bf16[1024,5,512]{2,0,1:T(8,128)(2,1)}), bf16[64,5,512]{2,0,1:T(8,128)(2,1)}) %reduce-scatter.5.cloned.1.call-update) | async-done | bytes 327696 | tf_op jit(solution)/shard_map/reduce_scatter | solution.py:39
  481.5 1.9 convert_element_type.91
  (42 shorter events, 11.9 us)
Async XLA Ops:
  7.2 104.3 %copy-start = (bf16[384,512]{1,0:T(8,128)(2,1)S(1)}, bf16[384,512]{1,0:T(8,128)(2,1)}, u32[]{:S(2)}) copy-start(bf16[384,512]{1,0:T(8,128)(2,1)} %param.7) | copy-start | bytes 1179652
  7.2 104.3 %all-gather.5.cloned.1.call-start = ((), (), s32[]{:S(2)}) async-start(), calls=%async_computation.3 | async-start | bytes 5570560 | tf_op jit(solution)/shard_map/all_gather | solution.py:51
  7.9 203.4 %all-gather.3.cloned.1.call-start = ((), (), s32[]{:S(2)}) async-start(), calls=%async_computation.2 | async-start | bytes 5570560 | tf_op jit(solution)/shard_map/all_gather | solution.py:50
  8.7 376.3 %reduce-scatter.3.cloned.1.call-start = ((), (), s32[]{:S(2)}) async-start(), calls=%async_computation.4 | async-start | bytes 8912896 | tf_op jit(solution)/shard_map/reduce_scatter | solution.py:26
  8.7 12.2 %collective-permute-start = (bf16[384,512]{1,0:T(8,128)(2,1)}, bf16[384,512]{1,0:T(8,128)(2,1)S(1)}, u32[]{:S(2)}, u32[]{:S(2)}) collective-permute-start(bf16[384,512]{1,0:T(8,128)(2,1)} %param.4), channel_id=1, source_target_pairs={{0,1},{1,0},{2,3},{3,2},{4,5},{5,4},{6,7},{7,6},{8,9},{9,8},{10,11... | collective-permute-start | bytes 1179656 | tf_op jit(solution)/shard_map/ppermute | solution.py:10
  8.8 12.9 %collective-permute-start.1 = (bf16[384,512]{1,0:T(8,128)(2,1)}, bf16[384,512]{1,0:T(8,128)(2,1)S(1)}, u32[]{:S(2)}, u32[]{:S(2)}) collective-permute-start(bf16[384,512]{1,0:T(8,128)(2,1)} %param.4), channel_id=1, source_target_pairs={{0,2},{1,3},{2,0},{3,1},{4,6},{5,7},{6,4},{7,5},{8,10},{9,11},{10,... | collective-permute-start | bytes 1179656 | tf_op jit(solution)/shard_map/ppermute | solution.py:10
  11.1 18.9 %collective-permute-start.2 = (bf16[384,512]{1,0:T(8,128)(2,1)}, bf16[384,512]{1,0:T(8,128)(2,1)S(1)}, u32[]{:S(2)}, u32[]{:S(2)}) collective-permute-start(bf16[384,512]{1,0:T(8,128)(2,1)} %param.4), channel_id=1, source_target_pairs={{0,4},{1,5},{2,6},{3,7},{4,0},{5,1},{6,2},{7,3},{8,12},{9,13},{10,... | collective-permute-start | bytes 1179656 | tf_op jit(solution)/shard_map/ppermute | solution.py:10
  11.9 114.3 %collective-permute-start.3 = (bf16[384,512]{1,0:T(8,128)(2,1)}, bf16[384,512]{1,0:T(8,128)(2,1)}, u32[]{:S(2)}, u32[]{:S(2)}) collective-permute-start(bf16[384,512]{1,0:T(8,128)(2,1)} %param.4), channel_id=1, source_target_pairs={{0,8},{1,9},{2,10},{3,11},{4,12},{5,13},{6,14},{7,15},{8,0},{9,1},... | collective-permute-start | bytes 1179656 | tf_op jit(solution)/shard_map/ppermute | solution.py:10
  117.9 100.2 %collective-permute-start.11 = (bf16[384,1024]{1,0:T(8,128)(2,1)}, bf16[384,1024]{1,0:T(8,128)(2,1)S(1)}, u32[]{:S(2)}, u32[]{:S(2)}) collective-permute-start(bf16[384,1024]{1,0:T(8,128)(2,1)} %get-tuple-element.15), channel_id=1, source_target_pairs={{0,8},{1,9},{2,10},{3,11},{4,12},{5,13},{6,14},{7,15},{8,0},{9,1},... | collective-permute-start | bytes 2359304 | tf_op jit(solution)/shard_map/ppermute | solution.py:10
  121.4 96.7 %collective-permute-start.10 = (bf16[384,1024]{1,0:T(8,128)(2,1)}, bf16[384,1024]{1,0:T(8,128)(2,1)S(1)}, u32[]{:S(2)}, u32[]{:S(2)}) collective-permute-start(bf16[384,1024]{1,0:T(8,128)(2,1)} %get-tuple-element.16), channel_id=1, source_target_pairs={{0,4},{1,5},{2,6},{3,7},{4,0},{5,1},{6,2},{7,3},{8,12},{9,13},{10,... | collective-permute-start | bytes 2359304 | tf_op jit(solution)/shard_map/ppermute | solution.py:10
  123.7 94.4 %collective-permute-start.9 = (bf16[384,1024]{1,0:T(8,128)(2,1)}, bf16[384,1024]{1,0:T(8,128)(2,1)S(1)}, u32[]{:S(2)}, u32[]{:S(2)}) collective-permute-start(bf16[384,1024]{1,0:T(8,128)(2,1)} %get-tuple-element.17), channel_id=1, source_target_pairs={{0,2},{1,3},{2,0},{3,1},{4,6},{5,7},{6,4},{7,5},{8,10},{9,11},{10,... | collective-permute-start | bytes 2359304 | tf_op jit(solution)/shard_map/ppermute | solution.py:10
  126.2 92.0 %collective-permute-start.8 = (bf16[384,1024]{1,0:T(8,128)(2,1)}, bf16[384,1024]{1,0:T(8,128)(2,1)}, u32[]{:S(2)}, u32[]{:S(2)}) collective-permute-start(bf16[384,1024]{1,0:T(8,128)(2,1)} %get-tuple-element.18), channel_id=1, source_target_pairs={{0,1},{1,0},{2,3},{3,2},{4,5},{5,4},{6,7},{7,6},{8,9},{9,8},{10,11... | collective-permute-start | bytes 2359304 | tf_op jit(solution)/shard_map/ppermute | solution.py:10
  218.1 0.9 copy-start.1
  240.0 1.1 copy-start.3
  240.1 241.4 %reduce-scatter.5.cloned.1.call-start = ((), (), s32[]{:S(2)}) async-start(), calls=%async_computation.5 | async-start | bytes 5570560 | tf_op jit(solution)/shard_map/reduce_scatter | solution.py:39
  241.2 5.6 %collective-permute-start.4 = (bf16[384,1024]{1,0:T(8,128)(2,1)S(1)}, bf16[384,1024]{1,0:T(8,128)(2,1)S(1)}, u32[]{:S(2)}, u32[]{:S(2)}) collective-permute-start(bf16[384,1024]{1,0:T(8,128)(2,1)S(1)} %copy-done.3), channel_id=1, source_target_pairs={{0,1},{1,0},{2,3},{3,2},{4,5},{5,4},{6,7},{7,6},{8,9},{9,8},{10,11... | collective-permute-start | bytes 2359304 | tf_op jit(solution)/shard_map/ppermute | solution.py:10
  241.2 20.4 %collective-permute-start.5 = (bf16[384,1024]{1,0:T(8,128)(2,1)S(1)}, bf16[384,1024]{1,0:T(8,128)(2,1)S(1)}, u32[]{:S(2)}, u32[]{:S(2)}) collective-permute-start(bf16[384,1024]{1,0:T(8,128)(2,1)S(1)} %copy-done.3), channel_id=1, source_target_pairs={{0,2},{1,3},{2,0},{3,1},{4,6},{5,7},{6,4},{7,5},{8,10},{9,11},{10,... | collective-permute-start | bytes 2359304 | tf_op jit(solution)/shard_map/ppermute | solution.py:10
  242.2 35.5 %collective-permute-start.6 = (bf16[384,1024]{1,0:T(8,128)(2,1)S(1)}, bf16[384,1024]{1,0:T(8,128)(2,1)S(1)}, u32[]{:S(2)}, u32[]{:S(2)}) collective-permute-start(bf16[384,1024]{1,0:T(8,128)(2,1)S(1)} %copy-done.3), channel_id=1, source_target_pairs={{0,4},{1,5},{2,6},{3,7},{4,0},{5,1},{6,2},{7,3},{8,12},{9,13},{10,... | collective-permute-start | bytes 2359304 | tf_op jit(solution)/shard_map/ppermute | solution.py:10
  243.0 51.7 %collective-permute-start.7 = (bf16[384,1024]{1,0:T(8,128)(2,1)S(1)}, bf16[384,1024]{1,0:T(8,128)(2,1)S(1)}, u32[]{:S(2)}, u32[]{:S(2)}) collective-permute-start(bf16[384,1024]{1,0:T(8,128)(2,1)S(1)} %copy-done.3), channel_id=1, source_target_pairs={{0,8},{1,9},{2,10},{3,11},{4,12},{5,13},{6,14},{7,15},{8,0},{9,1},... | collective-permute-start | bytes 2359304 | tf_op jit(solution)/shard_map/ppermute | solution.py:10
  307.3 7.8 %copy-start.2 = (bf16[384,5,1024]{2,0,1:T(8,128)(2,1)S(1)}, bf16[384,5,1024]{2,0,1:T(8,128)(2,1)}, u32[]{:S(2)}) copy-start(bf16[384,5,1024]{2,0,1:T(8,128)(2,1)} %bitcast_dynamic-update-slice_fusion) | copy-start | bytes 11796484
  307.5 29.0 %collective-permute-start.15 = (bf16[384,512]{1,0:T(8,128)(2,1)S(1)}, bf16[384,512]{1,0:T(8,128)(2,1)S(1)}, u32[]{:S(2)}, u32[]{:S(2)}) collective-permute-start(bf16[384,512]{1,0:T(8,128)(2,1)S(1)} %get-tuple-element.20), channel_id=1, source_target_pairs={{0,8},{1,9},{2,10},{3,11},{4,12},{5,13},{6,14},{7,15},{8,0},{9,1},... | collective-permute-start | bytes 1179656 | tf_op jit(solution)/shard_map/ppermute | solution.py:10
  312.3 24.2 %collective-permute-start.14 = (bf16[384,512]{1,0:T(8,128)(2,1)S(1)}, bf16[384,512]{1,0:T(8,128)(2,1)S(1)}, u32[]{:S(2)}, u32[]{:S(2)}) collective-permute-start(bf16[384,512]{1,0:T(8,128)(2,1)S(1)} %get-tuple-element.21), channel_id=1, source_target_pairs={{0,4},{1,5},{2,6},{3,7},{4,0},{5,1},{6,2},{7,3},{8,12},{9,13},{10,... | collective-permute-start | bytes 1179656 | tf_op jit(solution)/shard_map/ppermute | solution.py:10
  314.9 21.7 %collective-permute-start.13 = (bf16[384,512]{1,0:T(8,128)(2,1)S(1)}, bf16[384,512]{1,0:T(8,128)(2,1)S(1)}, u32[]{:S(2)}, u32[]{:S(2)}) collective-permute-start(bf16[384,512]{1,0:T(8,128)(2,1)S(1)} %get-tuple-element.22), channel_id=1, source_target_pairs={{0,2},{1,3},{2,0},{3,1},{4,6},{5,7},{6,4},{7,5},{8,10},{9,11},{10,... | collective-permute-start | bytes 1179656 | tf_op jit(solution)/shard_map/ppermute | solution.py:10
  315.1 21.4 %collective-permute-start.12 = (bf16[384,512]{1,0:T(8,128)(2,1)S(1)}, bf16[384,512]{1,0:T(8,128)(2,1)S(1)}, u32[]{:S(2)}, u32[]{:S(2)}) collective-permute-start(bf16[384,512]{1,0:T(8,128)(2,1)S(1)} %get-tuple-element.23), channel_id=1, source_target_pairs={{0,1},{1,0},{2,3},{3,2},{4,5},{5,4},{6,7},{7,6},{8,9},{9,8},{10,11... | collective-permute-start | bytes 1179656 | tf_op jit(solution)/shard_map/ppermute | solution.py:10
Sparse Core Ops, SparseCore 0:
  9.8 101.6 all-gather.4
  113.2 98.0 all-gather.2
  240.2 144.7 reduce-scatter.2
  387.4 94.0 reduce-scatter.4
where the time goes:
time: 491 us; the launch traced here: 490 us
  waiting for transfers between devices  376 us (77%)
  matrix products  34.8 us (7%)
  starting transfers between devices  32 us (7%)
  local copies, waits for them, and re-layouts  27.7 us (6%)
  between operations  13.9 us (3%)
  other arithmetic  5.79 us (1%)
    reduce_scatter x1, waiting for transfers between devices, reduce_out(): lax.psum_scatter(term(jnp.int32(0), lax.axis_size('dp') * shard_rows).ast...  94.4 us
    all_gather x1, waiting for transfers between devices, body(): lax.all_gather(weight_in, 'dp', axis=0, tiled=True)  83.3 us
    all_gather x1, waiting for transfers between devices, body(): lax.all_gather(weight_out, 'dp', axis=0, tiled=True)  80.7 us
    ppermute x16, waiting for transfers between devices, swapped(): return lax.ppermute(value, axis, pairs)  68.5 us
    reduce_scatter x1, waiting for transfers between devices, reduce_in(): lax.psum_scatter(term(jnp.int32(0), lax.axis_size('dp') * shard_rows).ast...  47.4 us
    ppermute x16, starting transfers between devices, swapped(): return lax.ppermute(value, axis, pairs)  31.9 us
    convert_element_type x1, local copies, waits for them, and re-layouts, reduce_in(): term(jnp.int32(0), lax.axis_size('dp') * shard_rows).astype(jnp.bfloat16)  11.9 us
    unnamed x16, local copies, waits for them, and re-layouts  11.1 us
  transfers between devices with their start and end apart: 20, of which 9 were waited for; matrix products, arithmetic and copies ran while one was open for 9% of the time, Pallas kernels for 0%

commit v1 on v0

--- a/solution.py
+++ b/solution.py
@@ -2,6 +2,19 @@
 import jax.numpy as jnp
 from jax import lax
 from jax.sharding import PartitionSpec as P
+from jax.lax import all_to_all, axis_size
+
+
+def _spread_gates(arr):
+    return jnp.concatenate(
+        all_to_all(
+            jnp.stack(tuple((arr for _ in range(axis_size("dp"))))),
+            axis_name="dp",
+            split_axis=0,
+            concat_axis=0,
+        ),
+        axis=0,
+    )
 
 
 def swapped(value, axis, distance):
@@ -47,7 +60,7 @@
 def body(inputs, weight_in, weight_out, cotangent):
     levels = lax.axis_size("block").bit_length() - 1
     weight_in_all, weight_out_all = (
-        lax.all_gather(weight_in, "dp", axis=0, tiled=True),
+        _spread_gates(weight_in),
         lax.all_gather(weight_out, "dp", axis=0, tiled=True),
     )
     pieces = [inputs]

time: 491 us -> 549 us (1.12)
  waiting for transfers between devices: 376 us -> 426 us
  local copies, waits for them, and re-layouts: 27.7 us -> 34.9 us
    all_gather x1 -> x0, waiting for transfers between devices: 83.3 us -> none  [body(): lax.all_gather(weight_in, 'dp', axis=0, tiled=True)]
    all_gather x1, waiting for transfers between devices: 80.7 us -> 146 us  [body(): lax.all_gather(weight_out, 'dp', axis=0, tiled=True)]
    reduce_scatter x1, waiting for transfers between devices: 47.4 us -> 110 us  [reduce_in(): lax.psum_scatter(term(jnp.int32(0), lax.axis_size('dp') * shard_rows).ast...]
    all_to_all x0 -> x1, starting transfers between devices: none -> 8.51 us  [_spread_gates(): all_to_all(jnp.stack(tuple((arr for _ in range(axis_size('dp'))))), axis_...]
    ppermute x16, starting transfers between devices: 31.9 us -> 23.7 us  [swapped(): return lax.ppermute(value, axis, pairs)]
    unnamed x16 -> x18, local copies, waits for them, and re-layouts: 11.1 us -> 11.2 us
  transfers between devices with their start and end apart: 20 -> 20, of which waited for: 9 -> 12; matrix products, arithmetic and copies ran while one was open for 9% -> 9% of each run, Pallas kernels for 0% -> 0%
where the time goes in v1:
time: 549 us; the launch traced here: 548 us
  waiting for transfers between devices  426 us (78%)
  local copies, waits for them, and re-layouts  34.9 us (6%)
  matrix products  34.6 us (6%)
  starting transfers between devices  32.4 us (6%)
  between operations  13.8 us (3%)
  other arithmetic  5.79 us (1%)
    all_gather x1, waiting for transfers between devices, body(): lax.all_gather(weight_out, 'dp', axis=0, tiled=True)  146 us
    reduce_scatter x1, waiting for transfers between devices, reduce_in(): lax.psum_scatter(term(jnp.int32(0), lax.axis_size('dp') * shard_rows).ast...  110 us
    reduce_scatter x1, waiting for transfers between devices, reduce_out(): lax.psum_scatter(term(jnp.int32(0), lax.axis_size('dp') * shard_rows).ast...  96.5 us
    ppermute x16, waiting for transfers between devices, swapped(): return lax.ppermute(value, axis, pairs)  73.5 us
    ppermute x16, starting transfers between devices, swapped(): return lax.ppermute(value, axis, pairs)  23.7 us
    convert_element_type x1, local copies, waits for them, and re-layouts, reduce_in(): term(jnp.int32(0), lax.axis_size('dp') * shard_rows).astype(jnp.bfloat16)  11.9 us
    unnamed x18, local copies, waits for them, and re-layouts  11.2 us
  transfers between devices with their start and end apart: 20, of which 12 were waited for; matrix products, arithmetic and copies ran while one was open for 9% of the time, Pallas kernels for 0%

profile of v1, /device:TPU:8, one launch (start us, length us, event | category | flops | bytes accessed | tf_op | source)
XLA Modules:
  0.0 547.8 jit_solution(13107108790677977177)
XLA Ops:
  7.9 3.9 stack.61
  11.8 8.5 %all-to-all-start = ((bf16[16,32,5,1024]{3,1,2,0:T(8,128)(2,1)}), bf16[16,32,5,1024]{3,1,2,0:T(8,128)(2,1)}, u32[]{:S(2)}, u32[]{:S(2)}) async-start(bf16[16,32,5,1024]{3,1,2,0:T(8,128)(2,1)} %stack.61), calls=%async_computation | async-start | bytes 10485760 | tf_op jit(solution)/shard_map/all_to_all | solution.py:10
  21.0 2.6 collective-permute-start.2
  23.6 4.5 collective-permute-start.3
  28.1 1.8 bitcast_dynamic-update-slice_fusion.9
  30.7 2.1 collective-permute-done.1
  33.6 8.1 %collective-permute-done.2 = bf16[384,512]{1,0:T(8,128)(2,1)S(1)} collective-permute-done((bf16[384,512]{1,0:T(8,128)(2,1)}, bf16[384,512]{1,0:T(8,128)(2,1)S(1)}, u32[]{:S(2)}, u32[]{:S(2)}) %collective-permute-start.2) | collective-permute-done | bytes 393248 | tf_op jit(solution)/shard_map/ppermute | solution.py:23
  42.4 146.0 %all-gather.2.cloned.1.call-done = bf16[1024,5,512]{2,0,1:T(8,128)(2,1)} async-done(((bf16[64,5,512]{2,0,1:T(8,128)(2,1)}), bf16[1024,5,512]{2,0,1:T(8,128)(2,1)}) %all-gather.2.cloned.1.call-update) | async-done | bytes 5242896 | tf_op jit(solution)/shard_map/all_gather | solution.py:64
  188.5 4.7 convert_bitcast_fusion.2
  193.2 1.8 slice_bitcast_fusion.4
  195.0 6.0 %collective-permute-start.11 = (bf16[384,1024]{1,0:T(8,128)(2,1)}, bf16[384,1024]{1,0:T(8,128)(2,1)S(1)}, u32[]{:S(2)}, u32[]{:S(2)}) collective-permute-start(bf16[384,1024]{1,0:T(8,128)(2,1)} %get-tuple-element.15), channel_id=1, source_target_pairs={{0,8},{1,9},{2,10},{3,11},{4,12},{5,13},{6,14},{7,15},{8,0},{9,1},... | collective-permute-start | bytes 2359304 | tf_op jit(solution)/shard_map/ppermute | solution.py:23
  201.1 2.3 collective-permute-start.10
  204.6 1.8 bitcast_dynamic-update-slice_fusion.5
  206.4 3.1 copy.12
  209.6 6.7 %bitcast_dynamic-update-slice_fusion.4 = (bf16[384,5,1024]{2,0,1:T(8,128)(2,1)}, bf16[384,1024]{1,0:T(8,128)(2,1)}, f32[384,1024,1]{1,0,2:T(8,128)S(1)}) fusion(bf16[384,5,512]{2,0,1:T(8,128)(2,1)} %bitcast_dynamic-update-slice_fusion.5, bf16[512,5,1024]{2,0,1:T(8,128)(2,1)S(1)} %bitcast.90), kind=kOutput, calls=%fused_computation.31 | convolution fusion | flops 2016804864 | bytes 10354688 | tf_op jit(solution)/shard_map/tkc,ckh->th/dot_general | solution.py:70
  216.3 6.9 %collective-permute-done.10 = bf16[384,1024]{1,0:T(8,128)(2,1)S(1)} collective-permute-done((bf16[384,1024]{1,0:T(8,128)(2,1)}, bf16[384,1024]{1,0:T(8,128)(2,1)S(1)}, u32[]{:S(2)}, u32[]{:S(2)}) %collective-permute-start.10) | collective-permute-done | bytes 786464 | tf_op jit(solution)/shard_map/ppermute | solution.py:23
  223.2 12.4 %collective-permute-done.9 = bf16[384,1024]{1,0:T(8,128)(2,1)S(1)} collective-permute-done((bf16[384,1024]{1,0:T(8,128)(2,1)}, bf16[384,1024]{1,0:T(8,128)(2,1)S(1)}, u32[]{:S(2)}, u32[]{:S(2)}) %collective-permute-start.9) | collective-permute-done | bytes 786464 | tf_op jit(solution)/shard_map/ppermute | solution.py:23
  236.5 2.9 fusion.6
  239.4 6.2 %convert_bitcast_fusion.1 = bf16[512,5,1024]{0,2,1:T(8,128)(2,1)} fusion(bf16[384,5,512]{2,0,1:T(8,128)(2,1)} %bitcast_dynamic-update-slice_fusion.5, bf16[384,1024]{1,0:T(8,128)(2,1)S(1)} %fusion.6), kind=kOutput, calls=%fused_computation.1 | convolution fusion | flops 2015887360 | bytes 7995392 | tf_op jit(solution)/shard_map/tkc,th->ckh/dot_general | solution.py:37
  245.6 11.9 %copy.15 = bf16[512,5,1024]{2,1,0:T(8,128)(2,1)} copy(bf16[512,5,1024]{0,2,1:T(8,128)(2,1)} %convert_bitcast_fusion.1) | data formatting | bytes 10485760 | tf_op jit(solution)/shard_map/convert_element_type | solution.py:40
  262.0 17.1 %collective-permute-done.5 = bf16[384,1024]{1,0:T(8,128)(2,1)S(1)} collective-permute-done((bf16[384,1024]{1,0:T(8,128)(2,1)S(1)}, bf16[384,1024]{1,0:T(8,128)(2,1)S(1)}, u32[]{:S(2)}, u32[]{:S(2)}) %collective-permute-start.5) | collective-permute-done | bytes 786464 | tf_op jit(solution)/shard_map/ppermute | solution.py:23
  280.0 14.4 %collective-permute-done.6 = bf16[384,1024]{1,0:T(8,128)(2,1)S(1)} collective-permute-done((bf16[384,1024]{1,0:T(8,128)(2,1)S(1)}, bf16[384,1024]{1,0:T(8,128)(2,1)S(1)}, u32[]{:S(2)}, u32[]{:S(2)}) %collective-permute-start.6) | collective-permute-done | bytes 786464 | tf_op jit(solution)/shard_map/ppermute | solution.py:23
  296.4 6.8 %convert_bitcast_fusion = bf16[1024,5,512]{2,0,1:T(8,128)(2,1)} fusion(bf16[384,5,1024]{2,0,1:T(8,128)(2,1)} %bitcast_dynamic-update-slice_fusion, bf16[384,512]{1,0:T(8,128)(2,1)S(1)} %copy-done), kind=kOutput, calls=%fused_computation | convolution fusion | flops 2015887360 | bytes 9568256 | tf_op jit(solution)/shard_map/tkh,tc->hkc/dot_general | solution.py:50
  303.2 4.7 convert_bitcast_fusion.3
  308.7 3.2 collective-permute-start.14
  313.2 5.4 fusion.10
  318.7 4.7 collective-permute-done.15
  323.4 6.7 %collective-permute-done.13 = bf16[384,512]{1,0:T(8,128)(2,1)S(1)} collective-permute-done((bf16[384,512]{1,0:T(8,128)(2,1)S(1)}, bf16[384,512]{1,0:T(8,128)(2,1)S(1)}, u32[]{:S(2)}, u32[]{:S(2)}) %collective-permute-start.13) | collective-permute-done | bytes 393248 | tf_op jit(solution)/shard_map/ppermute | solution.py:23
  331.1 109.6 %reduce-scatter.3.cloned.1.call-done = bf16[32,5,1024]{2,1,0:T(8,128)(2,1)} async-done(((bf16[512,5,1024]{2,1,0:T(8,128)(2,1)}), bf16[32,5,1024]{2,1,0:T(8,128)(2,1)}) %reduce-scatter.3.cloned.1.call-update) | async-done | bytes 327696 | tf_op jit(solution)/shard_map/reduce_scatter | solution.py:39
  440.7 2.1 copy.17
  442.9 96.5 %reduce-scatter.5.cloned.1.call-done = bf16[64,5,512]{2,0,1:T(8,128)(2,1)} async-done(((bf16[1024,5,512]{2,0,1:T(8,128)(2,1)}), bf16[64,5,512]{2,0,1:T(8,128)(2,1)}) %reduce-scatter.5.cloned.1.call-update) | async-done | bytes 327696 | tf_op jit(solution)/shard_map/reduce_scatter | solution.py:52
  539.4 1.9 convert_element_type.91
  (45 shorter events, 16.3 us)
Async XLA Ops:
  7.2 181.3 %copy-start = (bf16[384,512]{1,0:T(8,128)(2,1)S(1)}, bf16[384,512]{1,0:T(8,128)(2,1)}, u32[]{:S(2)}) copy-start(bf16[384,512]{1,0:T(8,128)(2,1)} %param.7) | copy-start | bytes 1179652
  7.2 181.3 %all-gather.2.cloned.1.call-start = ((), (), s32[]{:S(2)}) async-start(), calls=%async_computation.3 | async-start | bytes 5570560 | tf_op jit(solution)/shard_map/all_gather | solution.py:64
  11.8 194.6 %all-to-all-start = ((bf16[16,32,5,1024]{3,1,2,0:T(8,128)(2,1)}), bf16[16,32,5,1024]{3,1,2,0:T(8,128)(2,1)}, u32[]{:S(2)}, u32[]{:S(2)}) async-start(bf16[16,32,5,1024]{3,1,2,0:T(8,128)(2,1)} %stack.61), calls=%async_computation | async-start | bytes 10485760 | tf_op jit(solution)/shard_map/all_to_all | solution.py:10
  20.3 420.4 %reduce-scatter.3.cloned.1.call-start = ((), (), s32[]{:S(2)}) async-start(), calls=%async_computation.4 | async-start | bytes 8912896 | tf_op jit(solution)/shard_map/reduce_scatter | solution.py:39
  20.4 9.5 %collective-permute-start = (bf16[384,512]{1,0:T(8,128)(2,1)}, bf16[384,512]{1,0:T(8,128)(2,1)S(1)}, u32[]{:S(2)}, u32[]{:S(2)}) collective-permute-start(bf16[384,512]{1,0:T(8,128)(2,1)} %param.4), channel_id=1, source_target_pairs={{0,1},{1,0},{2,3},{3,2},{4,5},{5,4},{6,7},{7,6},{8,9},{9,8},{10,11... | collective-permute-start | bytes 1179656 | tf_op jit(solution)/shard_map/ppermute | solution.py:23
  20.5 12.3 %collective-permute-start.1 = (bf16[384,512]{1,0:T(8,128)(2,1)}, bf16[384,512]{1,0:T(8,128)(2,1)S(1)}, u32[]{:S(2)}, u32[]{:S(2)}) collective-permute-start(bf16[384,512]{1,0:T(8,128)(2,1)} %param.4), channel_id=1, source_target_pairs={{0,2},{1,3},{2,0},{3,1},{4,6},{5,7},{6,4},{7,5},{8,10},{9,11},{10,... | collective-permute-start | bytes 1179656 | tf_op jit(solution)/shard_map/ppermute | solution.py:23
  21.0 20.6 %collective-permute-start.2 = (bf16[384,512]{1,0:T(8,128)(2,1)}, bf16[384,512]{1,0:T(8,128)(2,1)S(1)}, u32[]{:S(2)}, u32[]{:S(2)}) collective-permute-start(bf16[384,512]{1,0:T(8,128)(2,1)} %param.4), channel_id=1, source_target_pairs={{0,4},{1,5},{2,6},{3,7},{4,0},{5,1},{6,2},{7,3},{8,12},{9,13},{10,... | collective-permute-start | bytes 1179656 | tf_op jit(solution)/shard_map/ppermute | solution.py:23
  23.6 181.0 %collective-permute-start.3 = (bf16[384,512]{1,0:T(8,128)(2,1)}, bf16[384,512]{1,0:T(8,128)(2,1)}, u32[]{:S(2)}, u32[]{:S(2)}) collective-permute-start(bf16[384,512]{1,0:T(8,128)(2,1)} %param.4), channel_id=1, source_target_pairs={{0,8},{1,9},{2,10},{3,11},{4,12},{5,13},{6,14},{7,15},{8,0},{9,1},... | collective-permute-start | bytes 1179656 | tf_op jit(solution)/shard_map/ppermute | solution.py:23
  195.0 21.2 %collective-permute-start.11 = (bf16[384,1024]{1,0:T(8,128)(2,1)}, bf16[384,1024]{1,0:T(8,128)(2,1)S(1)}, u32[]{:S(2)}, u32[]{:S(2)}) collective-permute-start(bf16[384,1024]{1,0:T(8,128)(2,1)} %get-tuple-element.15), channel_id=1, source_target_pairs={{0,8},{1,9},{2,10},{3,11},{4,12},{5,13},{6,14},{7,15},{8,0},{9,1},... | collective-permute-start | bytes 2359304 | tf_op jit(solution)/shard_map/ppermute | solution.py:23
  201.1 22.1 %collective-permute-start.10 = (bf16[384,1024]{1,0:T(8,128)(2,1)}, bf16[384,1024]{1,0:T(8,128)(2,1)S(1)}, u32[]{:S(2)}, u32[]{:S(2)}) collective-permute-start(bf16[384,1024]{1,0:T(8,128)(2,1)} %get-tuple-element.16), channel_id=1, source_target_pairs={{0,4},{1,5},{2,6},{3,7},{4,0},{5,1},{6,2},{7,3},{8,12},{9,13},{10,... | collective-permute-start | bytes 2359304 | tf_op jit(solution)/shard_map/ppermute | solution.py:23
  203.4 32.2 %collective-permute-start.9 = (bf16[384,1024]{1,0:T(8,128)(2,1)}, bf16[384,1024]{1,0:T(8,128)(2,1)S(1)}, u32[]{:S(2)}, u32[]{:S(2)}) collective-permute-start(bf16[384,1024]{1,0:T(8,128)(2,1)} %get-tuple-element.17), channel_id=1, source_target_pairs={{0,2},{1,3},{2,0},{3,1},{4,6},{5,7},{6,4},{7,5},{8,10},{9,11},{10,... | collective-permute-start | bytes 2359304 | tf_op jit(solution)/shard_map/ppermute | solution.py:23
  204.6 31.0 %collective-permute-start.8 = (bf16[384,1024]{1,0:T(8,128)(2,1)}, bf16[384,1024]{1,0:T(8,128)(2,1)}, u32[]{:S(2)}, u32[]{:S(2)}) collective-permute-start(bf16[384,1024]{1,0:T(8,128)(2,1)} %get-tuple-element.18), channel_id=1, source_target_pairs={{0,1},{1,0},{2,3},{3,2},{4,5},{5,4},{6,7},{7,6},{8,9},{9,8},{10,11... | collective-permute-start | bytes 2359304 | tf_op jit(solution)/shard_map/ppermute | solution.py:23
  209.5 6.7 %copy-start.1 = (bf16[16,32,5,1024]{3,1,0,2:T(8,128)(2,1)}, bf16[16,32,5,1024]{3,1,0,2:T(8,128)(2,1)S(1)}, u32[]{:S(2)}) copy-start(bf16[16,32,5,1024]{3,1,0,2:T(8,128)(2,1)S(1)} %copy.12) | copy-start | bytes 15728644
  235.6 0.9 copy-start.2
  257.5 1.1 copy-start.4
  257.6 281.8 %reduce-scatter.5.cloned.1.call-start = ((), (), s32[]{:S(2)}) async-start(), calls=%async_computation.5 | async-start | bytes 5570560 | tf_op jit(solution)/shard_map/reduce_scatter | solution.py:52
  258.7 2.3 collective-permute-start.4
  258.7 20.4 %collective-permute-start.5 = (bf16[384,1024]{1,0:T(8,128)(2,1)S(1)}, bf16[384,1024]{1,0:T(8,128)(2,1)S(1)}, u32[]{:S(2)}, u32[]{:S(2)}) collective-permute-start(bf16[384,1024]{1,0:T(8,128)(2,1)S(1)} %copy-done.4), channel_id=1, source_target_pairs={{0,2},{1,3},{2,0},{3,1},{4,6},{5,7},{6,4},{7,5},{8,10},{9,11},{10,... | collective-permute-start | bytes 2359304 | tf_op jit(solution)/shard_map/ppermute | solution.py:23
  259.4 35.1 %collective-permute-start.6 = (bf16[384,1024]{1,0:T(8,128)(2,1)S(1)}, bf16[384,1024]{1,0:T(8,128)(2,1)S(1)}, u32[]{:S(2)}, u32[]{:S(2)}) collective-permute-start(bf16[384,1024]{1,0:T(8,128)(2,1)S(1)} %copy-done.4), channel_id=1, source_target_pairs={{0,4},{1,5},{2,6},{3,7},{4,0},{5,1},{6,2},{7,3},{8,12},{9,13},{10,... | collective-permute-start | bytes 2359304 | tf_op jit(solution)/shard_map/ppermute | solution.py:23
  259.7 35.7 %collective-permute-start.7 = (bf16[384,1024]{1,0:T(8,128)(2,1)S(1)}, bf16[384,1024]{1,0:T(8,128)(2,1)S(1)}, u32[]{:S(2)}, u32[]{:S(2)}) collective-permute-start(bf16[384,1024]{1,0:T(8,128)(2,1)S(1)} %copy-done.4), channel_id=1, source_target_pairs={{0,8},{1,9},{2,10},{3,11},{4,12},{5,13},{6,14},{7,15},{8,0},{9,1},... | collective-permute-start | bytes 2359304 | tf_op jit(solution)/shard_map/ppermute | solution.py:23
  307.9 5.4 copy-start.3
  308.1 15.3 %collective-permute-start.15 = (bf16[384,512]{1,0:T(8,128)(2,1)S(1)}, bf16[384,512]{1,0:T(8,128)(2,1)S(1)}, u32[]{:S(2)}, u32[]{:S(2)}) collective-permute-start(bf16[384,512]{1,0:T(8,128)(2,1)S(1)} %get-tuple-element.20), channel_id=1, source_target_pairs={{0,8},{1,9},{2,10},{3,11},{4,12},{5,13},{6,14},{7,15},{8,0},{9,1},... | collective-permute-start | bytes 1179656 | tf_op jit(solution)/shard_map/ppermute | solution.py:23
  308.7 14.7 %collective-permute-start.14 = (bf16[384,512]{1,0:T(8,128)(2,1)S(1)}, bf16[384,512]{1,0:T(8,128)(2,1)S(1)}, u32[]{:S(2)}, u32[]{:S(2)}) collective-permute-start(bf16[384,512]{1,0:T(8,128)(2,1)S(1)} %get-tuple-element.21), channel_id=1, source_target_pairs={{0,4},{1,5},{2,6},{3,7},{4,0},{5,1},{6,2},{7,3},{8,12},{9,13},{10,... | collective-permute-start | bytes 1179656 | tf_op jit(solution)/shard_map/ppermute | solution.py:23
  311.9 18.2 %collective-permute-start.13 = (bf16[384,512]{1,0:T(8,128)(2,1)S(1)}, bf16[384,512]{1,0:T(8,128)(2,1)S(1)}, u32[]{:S(2)}, u32[]{:S(2)}) collective-permute-start(bf16[384,512]{1,0:T(8,128)(2,1)S(1)} %get-tuple-element.22), channel_id=1, source_target_pairs={{0,2},{1,3},{2,0},{3,1},{4,6},{5,7},{6,4},{7,5},{8,10},{9,11},{10,... | collective-permute-start | bytes 1179656 | tf_op jit(solution)/shard_map/ppermute | solution.py:23
  313.2 16.9 %collective-permute-start.12 = (bf16[384,512]{1,0:T(8,128)(2,1)S(1)}, bf16[384,512]{1,0:T(8,128)(2,1)S(1)}, u32[]{:S(2)}, u32[]{:S(2)}) collective-permute-start(bf16[384,512]{1,0:T(8,128)(2,1)S(1)} %get-tuple-element.23), channel_id=1, source_target_pairs={{0,1},{1,0},{2,3},{3,2},{4,5},{5,4},{6,7},{7,6},{8,9},{9,8},{10,11... | collective-permute-start | bytes 1179656 | tf_op jit(solution)/shard_map/ppermute | solution.py:23
Sparse Core Ops, SparseCore 0:
  9.8 178.6 all-gather.1
  257.7 183.0 reduce-scatter.2
  443.3 96.0 reduce-scatter.4
